TPU v7x, 512 devices: a whole 4x4x16 slice. The times are simulated.
512 devices in a mesh: dp: 4 (over z_hi, core), tm: 8 (over z_lo), height: 16 (over x, y).
Axes of the slice: x: 4, y: 4, z: 16 (z_hi: 2, z_lo: 8; z = z_hi * 8 + z_lo), core: 2. Of those that a mesh axis runs over, the one named last changes fastest.
Arguments:
- clips: bfloat16 [4, 16, 64, 128, 128], P('dp', 'tm', 'height'), may hold values from -6 to 6
- frame_counts: int32 [4, 5], P('dp'), may hold values from 1 to 9, 16 in all within a row
- conv_first: bfloat16 [3, 3, 3, 128, 128], replicated, may hold values from -0.109375 to 0.109375
- conv_down: bfloat16 [3, 3, 3, 128, 128], replicated, may hold values from -0.109375 to 0.109375
- out_cotangent: bfloat16 [4, 8, 32, 64, 128], P('dp', 'tm', 'height'), may hold values from -6 to 6
Outputs:
- encoded: bfloat16 [4, 8, 32, 64, 128], P('dp', 'tm', 'height')
- grad_first: bfloat16 [3, 3, 3, 128, 128], P(None, None, None, 'dp')
- grad_down: bfloat16 [3, 3, 3, 128, 128], P(None, None, None, 'dp')
Inputs may be any that keep to these rules, and one draw needn't show every extreme that they name: `frame_counts`: each sequence's 5 clip lengths sum to 16; in every sequence one clip has exactly 9 frames.
All inputs are finite; a program needn't handle non-finite values.
Results may differ from a plain program's by a relative error of at most 0.0059.
Values may be sent and summed in bfloat16 or wider, within the bound.
No kernel may reach another device: no remote copies, remote signals or barrier semaphores. Data moves between devices by JAX's collectives and lax.ppermute only.
A program may use at most 64 MiB of HBM per device.

v0:
```python
import math
import jax
import jax.numpy as jnp
from jax import lax
from jax.sharding import PartitionSpec as P


def padded_2(cells, sides, width):
    for axis, dim in sides:
        count = lax.axis_size(axis)
        ends = count - 1
        head = lax.slice_in_dim(cells, 0, width, axis=dim)
        tail = lax.slice_in_dim(cells, cells.shape[dim] - width, cells.shape[dim], axis=dim)
        cells = jnp.concatenate(
            [
                lax.ppermute(tail, axis, [(i, (i + 1) % count) for i in range(ends)]),
                cells,
                lax.ppermute(head, axis, [((i + 1) % count, i) for i in range(ends)]),
            ],
            axis=dim,
        )
    return cells


def shifted(value, axis, steps):
    count = lax.axis_size(axis)
    leading, last = (max(0, -steps), min(count, count - steps))
    return lax.ppermute(value, axis, [(source, source + steps) for source in range(leading, last)])


def unfold(frame_slab, stride, pad_cols):
    padded = jnp.pad(frame_slab, ((0, 0), (0, 0), pad_cols, (0, 0)))
    out_rows = (padded.shape[1] - 3) // stride + 1
    out_cols = (padded.shape[2] - 3) // stride + 1
    pieces = []
    for tap_row in range(3):
        for tap_col in range(3):
            pieces.append(
                padded[
                    :,
                    tap_row : tap_row + stride * (out_rows - 1) + 1 : stride,
                    tap_col : tap_col + stride * (out_cols - 1) + 1 : stride,
                ]
            )
    joined = jnp.concatenate(pieces, axis=-1)
    return (joined.reshape(-1, joined.shape[-1]), (frame_slab.shape[0], out_rows, out_cols))


def conv_layer(extended, weight, tap_mask, out_frames, stride, pad_cols):
    channels_out = weight.shape[-1]
    summed = None
    for tap_time in range(3):
        frame_slab = extended[tap_time : tap_time + stride * (out_frames - 1) + 1 : stride]
        columns, shape_out = unfold(frame_slab, stride, pad_cols)
        kernel = weight[tap_time].reshape(-1, channels_out)
        tap_term = jnp.dot(columns, kernel, preferred_element_type=jnp.float32).reshape(
            shape_out + (channels_out,)
        )
        tap_term = tap_term * tap_mask[:, tap_time][:, None, None, None]
        summed = tap_term if summed is None else summed + tap_term
    return summed


def weight_grad(extended, grads, tap_mask, stride, pad_cols):
    out_frames = grads.shape[0]
    blocks = []
    for tap_time in range(3):
        frame_slab = extended[tap_time : tap_time + stride * (out_frames - 1) + 1 : stride]
        columns, shape_out = unfold(frame_slab, stride, pad_cols)
        masked = grads * tap_mask[:, tap_time].astype(jnp.bfloat16)[:, None, None, None]
        blocks.append(
            jnp.dot(
                columns.T, masked.reshape(-1, grads.shape[-1]), preferred_element_type=jnp.float32
            )
        )
    stacked = jnp.stack(blocks)
    return stacked.reshape(3, 3, 3, extended.shape[-1], grads.shape[-1])


def hidden_grad(grads_ext, weight, mask_ext):
    pieces = []
    for tap_time in range(3):
        masked = grads_ext * mask_ext[:, tap_time].astype(jnp.bfloat16)[:, None, None, None]
        kernel = jnp.transpose(weight[tap_time][::-1, ::-1], (0, 1, 3, 2))
        spread = lax.conv_general_dilated(
            masked,
            kernel,
            (1, 1),
            ((2, 0), (2, 2)),
            lhs_dilation=(2, 2),
            dimension_numbers=("NHWC", "HWIO", "NHWC"),
            preferred_element_type=jnp.float32,
        )
        pieces.append(spread[:, 1:, 1:])
    even_frames = pieces[2][:-1] + pieces[0][1:]
    odd_frames = pieces[1][1:]
    merged = jnp.stack([even_frames, odd_frames], axis=1)
    return merged.reshape((2 * even_frames.shape[0],) + even_frames.shape[1:])


def positions(counts_row, frame_index):
    starts = jnp.cumsum(counts_row) - counts_row
    latest = jnp.max(jnp.where(starts[None, :] <= frame_index[:, None], starts[None, :], 0), axis=1)
    return frame_index - latest


def tap_masks(place):
    return (place[:, None] >= (2 - jnp.arange(3, dtype=jnp.int32))[None, :]).astype(jnp.float32)


def body(clips, frame_counts, conv_first, conv_down, out_cotangent):
    frames_dev = clips.shape[1]
    rows_dev = clips.shape[2]
    columns_all = clips.shape[3]
    down_frames = frames_dev // 2
    counts_row = frame_counts[0]
    first_frame = lax.axis_index("tm") * frames_dev
    frame_index = first_frame + jnp.arange(frames_dev, dtype=jnp.int32)
    first_mask = tap_masks(positions(counts_row, frame_index))
    down_index = first_frame + 2 * jnp.arange(down_frames + 1, dtype=jnp.int32)
    mask_ext = tap_masks(positions(counts_row, down_index))
    down_mask = mask_ext[:down_frames]
    with_rows = padded_2(clips[0], (("height", 1),), 1)
    earlier = shifted(with_rows, "tm", 1)
    input_ext = jnp.concatenate([earlier, with_rows], axis=0)
    pre_act = conv_layer(input_ext, conv_first, first_mask, frames_dev, 1, (1, 1))
    hidden = jax.nn.silu(pre_act).astype(jnp.bfloat16)
    above = shifted(hidden[:, rows_dev - 1 :], "height", 1)
    hidden_rows = jnp.concatenate([above, hidden], axis=1)
    hidden_past = shifted(hidden_rows, "tm", 1)
    hidden_ext = jnp.concatenate([hidden_past, hidden_rows], axis=0)
    encoded = conv_layer(hidden_ext, conv_down, down_mask, down_frames, 2, (1, 0)).astype(
        jnp.bfloat16
    )
    cells_all = (
        lax.axis_size("dp")
        * clips.shape[0]
        * down_frames
        * lax.axis_size("tm")
        * (rows_dev // 2)
        * lax.axis_size("height")
        * (columns_all // 2)
    )
    scale = 1.0 / math.sqrt(cells_all)
    grads = (out_cotangent[0].astype(jnp.float32) * scale).astype(jnp.bfloat16)
    down_local = weight_grad(hidden_ext, grads, down_mask, 2, (1, 0))
    below = shifted(grads[:, 0:1], "height", -1)
    grads_rows = jnp.concatenate([grads, below], axis=1)
    grads_next = shifted(grads_rows, "tm", -1)
    grads_ext = jnp.concatenate([grads_rows, grads_next], axis=0)
    back_hidden = hidden_grad(grads_ext, conv_down, mask_ext).astype(jnp.bfloat16)
    sigma = jax.nn.sigmoid(pre_act)
    pre_grad = (back_hidden.astype(jnp.float32) * sigma * (1.0 + pre_act * (1.0 - sigma))).astype(
        jnp.bfloat16
    )
    first_local = weight_grad(input_ext, pre_grad, first_mask, 1, (1, 1))
    share = conv_first.shape[3] // lax.axis_size("dp")
    summed_first, summed_down = lax.psum((first_local, down_local), ("dp", "tm", "height"))
    offset = lax.axis_index("dp") * share
    summed_first = lax.dynamic_slice_in_dim(summed_first, offset, share, 3)
    summed_down = lax.dynamic_slice_in_dim(summed_down, offset, share, 3)
    return (encoded[None], summed_first.astype(jnp.bfloat16), summed_down.astype(jnp.bfloat16))


def solution(mesh):
    in_specs = (
        P("dp", "tm", "height", None, None),
        P("dp", None),
        P(),
        P(),
        P("dp", "tm", "height", None, None),
    )
    out_specs = (
        P("dp", "tm", "height", None, None),
        P(None, None, None, "dp", None),
        P(None, None, None, "dp", None),
    )
    return jax.shard_map(body, mesh=mesh, in_specs=in_specs, out_specs=out_specs, check_vma=False)
```

profile of v0, /device:TPU:32, one launch (start us, length us, event | category | flops | bytes accessed | tf_op | source)
XLA Modules:
  0.0 263.5 jit_solution(3750914941561490961)
XLA Ops:
  0.6 1.0 fusion.93
  1.6 3.5 %collective-permute-start = (bf16[2,1,128,128]{3,2,1,0:T(8,128)(2,1)S(1)}, bf16[2,1,128,128]{3,2,1,0:T(8,128)(2,1)S(1)}, u32[]{:S(2)}, u32[]{:S(2)}) collective-permute-start(bf16[2,1,128,128]{3,2,1,0:T(8,128)(2,1)S(1)} %get-tuple-element.17), channel_id=1, source_target_pairs={{0,1},{1,2},{2,3},{3,4},{4,5},{5,6},{6,7},{7,8},{8,9},{9,10},{10,1... | collective-permute-start | bytes 196616 | tf_op jit(solution)/shard_map/ppermute | solution.py:16
  5.1 1.3 collective-permute-start.1
  6.4 0.8 fusion.63
  7.2 1.3 collective-permute-start.5
  8.5 0.8 reduce-window_clone.1
  9.4 0.7 subtract_bitcast_fusion
  10.4 1.2 fusion.91
  11.6 0.9 fusion.90
  13.1 0.6 slice.447
  13.7 0.6 slice.451
  16.0 5.2 %collective-permute-start.6 = (bf16[1,3,64,128]{3,2,1,0:T(8,128)(2,1)S(1)}, bf16[1,3,64,128]{3,2,1,0:T(8,128)(2,1)S(1)}, u32[]{:S(2)}, u32[]{:S(2)}) collective-permute-start(bf16[1,3,64,128]{3,2,1,0:T(8,128)(2,1)S(1)} %pad_maximum_fusion.7), channel_id=1, source_target_pairs={{16,0},{32,16},{48,32},{64,48},{80,64},{96,80},{112,96},{17,1},{33... | collective-permute-start | bytes 147464 | tf_op jit(solution)/shard_map/ppermute | solution.py:28
  21.3 1.9 collective-permute-start.2
  23.4 1.3 multiply_bitcast_fusion.1
  27.2 3.8 %collective-permute-done.2 = bf16[2,6,128,128]{3,2,1,0:T(8,128)(2,1)S(1)} collective-permute-done((bf16[2,6,128,128]{3,2,1,0:T(8,128)(2,1)S(1)}, bf16[2,6,128,128]{3,2,1,0:T(8,128)(2,1)S(1)}, u32[]{:S(2)}, u32[]{:S(2)}) %collective-permute-start.2) | collective-permute-done | bytes 393248 | tf_op jit(solution)/shard_map/ppermute | solution.py:28
  32.0 0.8 convolution_multiply_fusion.1
  33.7 0.8 fusion.1
  34.5 0.9 fusion.10
  35.5 5.2 %collective-permute-start.3 = (bf16[2,1,128,128]{3,2,1,0:T(8,128)(2,1)S(1)}, bf16[2,1,128,128]{3,2,1,0:T(8,128)(2,1)S(1)}, u32[]{:S(2)}, u32[]{:S(2)}) collective-permute-start(bf16[2,1,128,128]{3,2,1,0:T(8,128)(2,1)S(1)} %slice.437), channel_id=1, source_target_pairs={{0,1},{1,2},{2,3},{3,4},{4,5},{5,6},{6,7},{7,8},{8,9},{9,10},{10,1... | collective-permute-start | bytes 196616 | tf_op jit(solution)/shard_map/ppermute | solution.py:28
  40.7 0.9 fusion.26
  41.5 0.9 fusion.24
  42.4 0.9 fusion.22
  44.8 3.2 %collective-permute-start.4 = (bf16[2,5,128,128]{3,2,1,0:T(8,128)(2,1)S(1)}, bf16[2,5,128,128]{3,2,1,0:T(8,128)(2,1)S(1)}, u32[]{:S(2)}, u32[]{:S(2)}) collective-permute-start(bf16[2,5,128,128]{3,2,1,0:T(8,128)(2,1)S(1)} %pad_maximum_fusion.2), channel_id=1, source_target_pairs={{0,16},{16,32},{32,48},{48,64},{64,80},{80,96},{96,112},{1,17},{17... | collective-permute-start | bytes 983048 | tf_op jit(solution)/shard_map/ppermute | solution.py:28
  48.3 1.1 convolution_bitcast_fusion
  49.4 4.4 %collective-permute-done.4 = bf16[2,5,128,128]{3,2,1,0:T(8,128)(2,1)S(1)} collective-permute-done((bf16[2,5,128,128]{3,2,1,0:T(8,128)(2,1)S(1)}, bf16[2,5,128,128]{3,2,1,0:T(8,128)(2,1)S(1)}, u32[]{:S(2)}, u32[]{:S(2)}) %collective-permute-start.4) | collective-permute-done | bytes 327712 | tf_op jit(solution)/shard_map/ppermute | solution.py:28
  57.8 1.2 pad_maximum_fusion.1
  58.9 196.0 %all-reduce.8 = (bf16[3,3,3,128,128]{4,3,2,1,0:T(8,128)(2,1)}, bf16[3,3,3,128,128]{4,3,2,1,0:T(8,128)(2,1)}) all-reduce(f32[3,3,3,128,128]{4,3,2,1,0:T(8,128)S(1)} %pad_maximum_fusion, f32[3,3,3,128,128]{4,3,2,1,0:T(8,128)S(1)} %pad_maximum_fusion.1), channel_id=1, replica_groups=mesh['dp'=4,'tm'=8,'height'=16] {'dp','tm','height'}, use_global_device_ids=true, to_apply=%region_3.4 | all-reduce | flops 884736 | bytes 5308416 | tf_op jit(solution)/shard_map/psum | solution.py:158
  255.0 1.7 dynamic-slice_convert_fusion
  256.7 1.6 dynamic-slice_convert_fusion.1
  258.3 1.8 convolution_multiply_fusion.5
  260.1 1.9 fusion.6
  262.1 1.4 fusion.8
  (154 shorter events, 10.4 us)
Async XLA Ops:
  0.6 20.6 %copy-start = (bf16[1,2,4,128,128]{4,3,2,1,0:T(8,128)(2,1)S(1)}, bf16[1,2,4,128,128]{4,3,2,1,0:T(8,128)(2,1)}, u32[]{:S(2)}) copy-start(bf16[1,2,4,128,128]{4,3,2,1,0:T(8,128)(2,1)} %param.5) | copy-start | bytes 786436
  0.6 10.9 %copy-start.6 = (bf16[3,3,3,128,128]{4,3,2,1,0:T(8,128)(2,1)S(1)}, bf16[3,3,3,128,128]{4,3,2,1,0:T(8,128)(2,1)}, u32[]{:S(2)}) copy-start(bf16[3,3,3,128,128]{4,3,2,1,0:T(8,128)(2,1)} %param.8) | copy-start | bytes 2654212
  1.6 19.6 %collective-permute-start = (bf16[2,1,128,128]{3,2,1,0:T(8,128)(2,1)S(1)}, bf16[2,1,128,128]{3,2,1,0:T(8,128)(2,1)S(1)}, u32[]{:S(2)}, u32[]{:S(2)}) collective-permute-start(bf16[2,1,128,128]{3,2,1,0:T(8,128)(2,1)S(1)} %get-tuple-element.17), channel_id=1, source_target_pairs={{0,1},{1,2},{2,3},{3,4},{4,5},{5,6},{6,7},{7,8},{8,9},{9,10},{10,1... | collective-permute-start | bytes 196616 | tf_op jit(solution)/shard_map/ppermute | solution.py:16
  5.1 16.1 %collective-permute-start.1 = (bf16[2,1,128,128]{3,2,1,0:T(8,128)(2,1)S(1)}, bf16[2,1,128,128]{3,2,1,0:T(8,128)(2,1)S(1)}, u32[]{:S(2)}, u32[]{:S(2)}) collective-permute-start(bf16[2,1,128,128]{3,2,1,0:T(8,128)(2,1)S(1)} %get-tuple-element.18), channel_id=1, source_target_pairs={{1,0},{2,1},{3,2},{4,3},{5,4},{6,5},{7,6},{8,7},{9,8},{10,9},{11,1... | collective-permute-start | bytes 196616 | tf_op jit(solution)/shard_map/ppermute | solution.py:18
  7.2 8.8 %collective-permute-start.5 = (bf16[1,1,64,128]{3,2,1,0:T(8,128)(2,1)S(1)}, bf16[1,1,64,128]{3,2,1,0:T(8,128)(2,1)S(1)}, u32[]{:S(2)}, u32[]{:S(2)}) collective-permute-start(bf16[1,1,64,128]{3,2,1,0:T(8,128)(2,1)S(1)} %slice.442), channel_id=1, source_target_pairs={{1,0},{2,1},{3,2},{4,3},{5,4},{6,5},{7,6},{8,7},{9,8},{10,9},{11,1... | collective-permute-start | bytes 49160 | tf_op jit(solution)/shard_map/ppermute | solution.py:28
  11.6 13.5 %copy-start.8 = (pred[8,18]{0,1:T(8,128)(4,1)S(1)}, pred[8,18]{0,1:T(8,128)(4,1)}, u32[]{:S(2)}) copy-start(pred[8,18]{0,1:T(8,128)(4,1)} %constant.62) | copy-start | bytes 436
  16.0 7.3 %collective-permute-start.6 = (bf16[1,3,64,128]{3,2,1,0:T(8,128)(2,1)S(1)}, bf16[1,3,64,128]{3,2,1,0:T(8,128)(2,1)S(1)}, u32[]{:S(2)}, u32[]{:S(2)}) collective-permute-start(bf16[1,3,64,128]{3,2,1,0:T(8,128)(2,1)S(1)} %pad_maximum_fusion.7), channel_id=1, source_target_pairs={{16,0},{32,16},{48,32},{64,48},{80,64},{96,80},{112,96},{17,1},{33... | collective-permute-start | bytes 147464 | tf_op jit(solution)/shard_map/ppermute | solution.py:28
  21.3 9.7 %collective-permute-start.2 = (bf16[2,6,128,128]{3,2,1,0:T(8,128)(2,1)S(1)}, bf16[2,6,128,128]{3,2,1,0:T(8,128)(2,1)S(1)}, u32[]{:S(2)}, u32[]{:S(2)}) collective-permute-start(bf16[2,6,128,128]{3,2,1,0:T(8,128)(2,1)S(1)} %pad_maximum_fusion.3), channel_id=1, source_target_pairs={{0,16},{16,32},{32,48},{48,64},{64,80},{80,96},{96,112},{1,17},{17... | collective-permute-start | bytes 1179656 | tf_op jit(solution)/shard_map/ppermute | solution.py:28
  35.5 8.0 %collective-permute-start.3 = (bf16[2,1,128,128]{3,2,1,0:T(8,128)(2,1)S(1)}, bf16[2,1,128,128]{3,2,1,0:T(8,128)(2,1)S(1)}, u32[]{:S(2)}, u32[]{:S(2)}) collective-permute-start(bf16[2,1,128,128]{3,2,1,0:T(8,128)(2,1)S(1)} %slice.437), channel_id=1, source_target_pairs={{0,1},{1,2},{2,3},{3,4},{4,5},{5,6},{6,7},{7,8},{8,9},{9,10},{10,1... | collective-permute-start | bytes 196616 | tf_op jit(solution)/shard_map/ppermute | solution.py:28
  43.5 4.9 %copy-start.7 = (bf16[1,1,2,64,128]{4,3,2,1,0:T(8,128)(2,1)S(1)}, bf16[1,1,2,64,128]{4,3,2,1,0:T(8,128)(2,1)}, u32[]{:S(2)}) copy-start(bf16[1,1,2,64,128]{4,3,2,1,0:T(8,128)(2,1)} %param.9) | copy-start | bytes 98308
  44.8 9.0 %collective-permute-start.4 = (bf16[2,5,128,128]{3,2,1,0:T(8,128)(2,1)S(1)}, bf16[2,5,128,128]{3,2,1,0:T(8,128)(2,1)S(1)}, u32[]{:S(2)}, u32[]{:S(2)}) collective-permute-start(bf16[2,5,128,128]{3,2,1,0:T(8,128)(2,1)S(1)} %pad_maximum_fusion.2), channel_id=1, source_target_pairs={{0,16},{16,32},{32,48},{48,64},{64,80},{80,96},{96,112},{1,17},{17... | collective-permute-start | bytes 983048 | tf_op jit(solution)/shard_map/ppermute | solution.py:28
  48.2 8.4 %copy-start.1 = (bf16[1,2,64,1152]{3,2,1,0:T(8,128)(2,1)}, bf16[1,2,64,1152]{3,2,1,0:T(8,128)(2,1)S(1)}, u32[]{:S(2)}) copy-start(bf16[1,2,64,1152]{3,2,1,0:T(8,128)(2,1)S(1)} %constant_dynamic-update-slice_fusion.19) | copy-start | bytes 884740
  56.5 0.7 copy-start.3
  56.8 0.7 copy-start.4
  255.0 7.1 %copy-start.2 = (bf16[1,2,64,1152]{3,2,1,0:T(8,128)(2,1)S(1)}, bf16[1,2,64,1152]{3,2,1,0:T(8,128)(2,1)}, u32[]{:S(2)}) copy-start(bf16[1,2,64,1152]{3,2,1,0:T(8,128)(2,1)} %copy-done.1) | copy-start | bytes 884740
  255.0 7.1 %copy-start.5 = (bf16[1,3,3,128,128]{4,3,2,1,0:T(8,128)(2,1)S(1)}, bf16[1,3,3,128,128]{4,3,2,1,0:T(8,128)(2,1)}, u32[]{:S(2)}) copy-start(bf16[1,3,3,128,128]{4,3,2,1,0:T(8,128)(2,1)} %get-tuple-element.7) | copy-start | bytes 884740
where the time goes:
time: 264 us; the launch traced here: 263 us
  blocking collectives  196 us (74%)
  starting transfers between devices  21.6 us (8%)
  local copies, waits for them, and re-layouts  15.7 us (6%)
  matrix products  12.9 us (5%)
  waiting for transfers between devices  8.16 us (3%)
  other arithmetic  5.58 us (2%)
  between operations  3.58 us (1%)
    psum x1, blocking collectives, body(): lax.psum((first_local, down_local), ('dp', 'tm', 'height'))  196 us
    ppermute x5, starting transfers between devices, shifted(): lax.ppermute(value, axis, [(source, source + steps) for source in range(l...  16.8 us
    ppermute x5, waiting for transfers between devices, shifted(): lax.ppermute(value, axis, [(source, source + steps) for source in range(l...  8.16 us
    dot_general x6, matrix products, conv_layer(): jnp.dot(columns, kernel, preferred_element_type=jnp.float32)  7.65 us
  transfers between devices with their start and end apart: 7, of which 2 were waited for; matrix products, arithmetic and copies ran while one was open for 5% of the time, Pallas kernels for 0%

commit v1 on v0

--- a/solution.py
+++ b/solution.py
@@ -155,7 +155,9 @@
     )
     first_local = weight_grad(input_ext, pre_grad, first_mask, 1, (1, 1))
     share = conv_first.shape[3] // lax.axis_size("dp")
-    summed_first, summed_down = lax.psum((first_local, down_local), ("dp", "tm", "height"))
+    summed_first, summed_down = lax.psum(
+        lax.psum((first_local, down_local), axis_name=("tm", "height")), axis_name="dp"
+    )
     offset = lax.axis_index("dp") * share
     summed_first = lax.dynamic_slice_in_dim(summed_first, offset, share, 3)
     summed_down = lax.dynamic_slice_in_dim(summed_down, offset, share, 3)

time: 264 us -> 2210 us (8.37)
  the two profiles are of different devices: /device:TPU:32 before, /device:TPU:1 now
where the time goes in v1:
time: 2210 us
  waiting for transfers between devices  1940 us (88%)
  blocking collectives  203 us (9%)
    psum x1, waiting for transfers between devices, body(): lax.psum((first_local, down_local), axis_name=('tm', 'height'))  1940 us
    psum x1, blocking collectives, body(): lax.psum(lax.psum((first_local, down_local), axis_name=('tm', 'height')),...  203 us
  transfers between devices with their start and end apart: 8, of which 3 were waited for; matrix products, arithmetic and copies ran while one was open for 1% of the time, Pallas kernels for 0%

profile of v1, /device:TPU:1, one launch (start us, length us, event | category | flops | bytes accessed | tf_op | source)
XLA Modules:
  0.0 2213.9 jit_solution(9726102489325543180)
XLA Ops:
  7.2 0.9 fusion.93
  8.1 4.0 collective-permute-start
  12.2 1.3 collective-permute-start.1
  13.5 0.8 fusion.63
  14.3 1.3 collective-permute-start.5
  15.6 0.8 reduce-window_clone.1
  16.4 0.7 subtract_bitcast_fusion
  17.4 1.3 fusion.91
  18.7 0.6 fusion.94
  19.3 0.6 slice.447
  22.4 1.3 collective-permute-start.6
  23.8 4.2 collective-permute-start.2
  28.1 1.3 multiply_bitcast_fusion.1
  32.0 0.7 collective-permute-done.2
  33.8 0.8 convolution_multiply_fusion.1
  35.4 0.8 fusion.1
  36.2 0.9 fusion.10
  37.2 4.6 collective-permute-start.3
  41.8 0.9 fusion.26
  42.7 0.9 fusion.24
  43.6 0.9 fusion.22
  44.4 1.4 pad_maximum_fusion
  47.1 4.8 collective-permute-start.4
  52.5 3.3 collective-permute-done.4
  59.4 1.4 pad_maximum_fusion.1
  60.9 0.8 convolution_multiply_fusion.5
  61.7 0.9 fusion.6
  62.6 1.5 fusion.8
  64.1 1938.4 %all-reduce.11.cloned.1.call-done = (f32[3,3,3,128,128]{4,3,2,1,0:T(8,128)}, f32[3,3,3,128,128]{4,3,2,1,0:T(8,128)}) async-done(((f32[3,3,3,128,128]{4,3,2,1,0:T(8,128)}, f32[3,3,3,128,128]{4,3,2,1,0:T(8,128)}), (f32[3,3,3,128,128]{4,3,2,1,0:T(8,128)}, f32[3,3,3,128,128]{4,3,2,1,0:T(8,128)})) %all-reduce.11.cloned.1.call-update) | async-done | bytes 3538960 | tf_op jit(solution)/shard_map/psum | solution.py:159
  2002.5 203.2 %all-reduce.12 = (bf16[3,3,3,128,128]{4,3,2,1,0:T(8,128)(2,1)S(1)}, bf16[3,3,3,128,128]{4,3,2,1,0:T(8,128)(2,1)S(1)}) all-reduce(f32[3,3,3,128,128]{4,3,2,1,0:T(8,128)} %get-tuple-element.5, f32[3,3,3,128,128]{4,3,2,1,0:T(8,128)} %get-tuple-element.6), channel_id=1, replica_groups=mesh['dp'=4,'tm'=8,'height'=16] {'dp'}, use_global_device_ids=true, to_apply=%region_4.5 | all-reduce | flops 884736 | bytes 5308416 | tf_op jit(solution)/shard_map/psum | solution.py:158
  2205.7 0.7 dynamic-slice_convert_fusion
  2206.4 0.7 dynamic-slice_convert_fusion.1
  (147 shorter events, 10.3 us)
Async XLA Ops:
  7.2 16.6 copy-start
  7.2 1995.3 %all-reduce.11.cloned.1.call-start = ((), (), s32[]{:S(2)}) async-start(), calls=%async_computation | async-start | bytes 7077888 | tf_op jit(solution)/shard_map/psum | solution.py:159
  8.1 15.6 collective-permute-start
  12.2 11.6 collective-permute-start.1
  14.3 8.2 collective-permute-start.5
  17.4 12.4 copy-start.1
  17.4 12.4 copy-start.3
  22.4 5.7 collective-permute-start.6
  23.8 8.9 collective-permute-start.2
  37.2 8.6 collective-permute-start.3
  45.8 6.4 copy-start.2
  47.1 8.6 collective-permute-start.4
Sparse Core Ops, SparseCore 0:
  60.9 1941.4 all-reduce.10
